TPU v7x, 32 devices: a whole 2x2x4 slice. The times are simulated.
32 devices in a mesh: gx: 8 (over z, x), gy: 4 (over y, core).
Axes of the slice: x: 2, y: 2, z: 4, core: 2. Of those that a mesh axis runs over, the one named last changes fastest.
Arguments:
- inputs: bfloat16 [3, 256, 8192], P(None, 'gy', 'gx'), may hold values from -600 to 600
- norm_gain: bfloat16 [8192], P('gx'), may hold values from 0.099609375 to 1.8984375
- query_weight: bfloat16 [8192, 8192], P('gx', 'gy'), may hold values from -0.0625 to 0.0625
- key_weight: bfloat16 [8192, 1024], P('gx', 'gy'), may hold values from -0.0625 to 0.0625
- value_weight: bfloat16 [8192, 1024], P('gx', 'gy'), may hold values from -0.0625 to 0.0625
- output_weight: bfloat16 [8192, 8192], P('gy', 'gx'), may hold values from -0.0625 to 0.0625
- query_down: bfloat16 [256, 8192, 64], P('gy', 'gx'), may hold values from -0.0625 to 0.0625
- query_up: bfloat16 [256, 64, 8192], P('gx', None, 'gy'), may hold values from -0.75 to 0.75
- output_down: bfloat16 [256, 8192, 64], P('gx', 'gy'), may hold values from -0.0625 to 0.0625
- output_up: bfloat16 [256, 64, 8192], P('gy', None, 'gx'), may hold values from -0.75 to 0.75
- block_adapter: int32 [2], replicated, may hold values from 0 to 255
- cache_lengths: int32 [256], P(('gx', 'gy')), may hold values from 1 to 256, as said below
- cache_keys: bfloat16 [256, 256, 1024], P(('gx', 'gy')), may hold values from -160 to 160
- cache_values: bfloat16 [256, 256, 1024], P(('gx', 'gy')), may hold values from -6 to 6
Outputs:
- block_output: bfloat16 [3, 256, 8192], P(None, 'gy', 'gx')
Inputs may be any that keep to these rules, and one draw needn't show every extreme that they name: `cache_lengths`: some request has exactly 256 cached positions.
All inputs are finite; a program needn't handle non-finite values.
Results may differ from a plain program's by a relative error of at most 0.012.
The roundings to bfloat16 on the way count: a program that leaves them out, or rounds other values in their place, can miss the bound.
Values may be sent and summed in bfloat16 or wider, within the bound.
No kernel may reach another device: no remote copies, remote signals or barrier semaphores. Data moves between devices by JAX's collectives and lax.ppermute only.
A program may use at most 192 MiB of HBM per device.

v0:
```python
import jax
import jax.numpy as jnp
from jax import lax
from jax.sharding import PartitionSpec as P

QUERY_HEADS = 64
KEY_VALUE_HEADS = 8
HEAD_FEATURES = 128
BLOCK = 128
EPS = 1e-05
THETA = 500000.0


def rotary_embedding(values_in, token_positions):
    half_size = values_in.shape[-1] // 2
    exponent = jnp.arange(half_size, dtype=jnp.float32) * 2.0 / values_in.shape[-1]
    frequency = THETA ** (-exponent)
    angles = token_positions.astype(jnp.float32)[:, None] * frequency[None, :]
    cosine = jnp.cos(angles)[:, None, :]
    sine_part = jnp.sin(angles)[:, None, :]
    lower = values_in[..., :half_size]
    upper = values_in[..., half_size:]
    return jnp.concatenate(
        [lower * cosine - upper * sine_part, upper * cosine + lower * sine_part], axis=-1
    )


def pick_adapters(table, adapter_ids, owner_index):
    table_count = table.shape[0]
    picked = []
    for block in range(adapter_ids.shape[0]):
        wanted = adapter_ids[block]
        owned = wanted // table_count == owner_index
        entry = lax.dynamic_index_in_dim(table, wanted % table_count, axis=0, keepdims=False)
        picked.append(jnp.where(owned, entry, jnp.zeros_like(entry)))
    return jnp.stack(picked)


def attend(query_rows, previous_keys, previous_values, incoming_keys, incoming_values, lengths):
    steps, count_of_rows = (query_rows.shape[0], query_rows.shape[1])
    groups = QUERY_HEADS // KEY_VALUE_HEADS
    context_window = previous_keys.shape[1]
    grouped_heads = (
        query_rows.reshape(steps, count_of_rows, KEY_VALUE_HEADS, groups, HEAD_FEATURES)
        .transpose(1, 2, 0, 3, 4)
        .reshape(count_of_rows, KEY_VALUE_HEADS, steps * groups, HEAD_FEATURES)
    )
    keys_previous = previous_keys.reshape(
        count_of_rows, context_window, KEY_VALUE_HEADS, HEAD_FEATURES
    )
    values_previous = previous_values.reshape(
        count_of_rows, context_window, KEY_VALUE_HEADS, HEAD_FEATURES
    )
    keys_incoming = incoming_keys.reshape(
        steps, count_of_rows, KEY_VALUE_HEADS, HEAD_FEATURES
    ).transpose(1, 0, 2, 3)
    values_incoming = incoming_values.reshape(
        steps, count_of_rows, KEY_VALUE_HEADS, HEAD_FEATURES
    ).transpose(1, 0, 2, 3)
    factor = HEAD_FEATURES ** (-0.5)
    score_old = (
        jnp.einsum(
            "rhqd,rchd->rhqc", grouped_heads, keys_previous, preferred_element_type=jnp.float32
        )
        * factor
    )
    score_new = (
        jnp.einsum(
            "rhqd,rshd->rhqs", grouped_heads, keys_incoming, preferred_element_type=jnp.float32
        )
        * factor
    )
    live_old = (jnp.arange(context_window, dtype=jnp.int32)[None, :] < lengths[:, None])[
        :, None, None, :
    ]
    query_step = jnp.arange(steps * groups, dtype=jnp.int32) // groups
    live_new = (jnp.arange(steps, dtype=jnp.int32)[None, :] <= query_step[:, None])[
        None, None, :, :
    ]
    score_old = jnp.where(live_old, score_old, -1e30)
    score_new = jnp.where(live_new, score_new, -1e30)
    peak_score = jnp.maximum(jnp.max(score_old, axis=-1), jnp.max(score_new, axis=-1))
    weight_old = jnp.where(live_old, jnp.exp(score_old - peak_score[..., None]), 0.0)
    weight_new = jnp.where(live_new, jnp.exp(score_new - peak_score[..., None]), 0.0)
    weight_sum = jnp.sum(weight_old, axis=-1) + jnp.sum(weight_new, axis=-1)
    mixed_out = jnp.einsum(
        "rhqc,rchd->rhqd",
        weight_old.astype(jnp.bfloat16),
        values_previous,
        preferred_element_type=jnp.float32,
    )
    mixed_out = mixed_out + jnp.einsum(
        "rhqs,rshd->rhqd",
        weight_new.astype(jnp.bfloat16),
        values_incoming,
        preferred_element_type=jnp.float32,
    )
    mixed_out = (mixed_out / weight_sum[..., None]).astype(jnp.bfloat16)
    return (
        mixed_out.reshape(count_of_rows, KEY_VALUE_HEADS, steps, groups, HEAD_FEATURES)
        .transpose(2, 0, 1, 3, 4)
        .reshape(steps, count_of_rows, -1)
    )


def local(
    inputs,
    norm_gain,
    query_weight,
    key_weight,
    value_weight,
    output_weight,
    query_down,
    query_up,
    output_down,
    output_up,
    block_adapter,
    cache_lengths,
    cache_keys,
    cache_values,
):
    across_first = lax.axis_size("gx")
    across_second = lax.axis_size("gy")
    index_first = lax.axis_index("gx")
    index_second = lax.axis_index("gy")
    steps = inputs.shape[0]
    request_count = inputs.shape[1] * across_second
    width = inputs.shape[2] * across_first
    local_rows = cache_keys.shape[0]
    block_count = block_adapter.shape[0]
    block_rows = request_count // block_count
    query_width = query_weight.shape[1]
    key_width = key_weight.shape[1]
    norm_scale = norm_gain.astype(jnp.float32)
    query_first = pick_adapters(query_down, block_adapter, index_second)
    query_second = pick_adapters(query_up, block_adapter, index_first)
    output_first = pick_adapters(output_down, block_adapter, index_first)
    output_second = pick_adapters(output_up, block_adapter, index_second)
    rows_all = lax.all_gather(inputs, "gy", axis=1, tiled=True)
    rows_wide = rows_all.astype(jnp.float32)
    squares = lax.psum(jnp.sum(rows_wide * rows_wide, axis=2), "gx")
    factor_rows = lax.rsqrt(squares / width + EPS)
    normed = (rows_wide * factor_rows[..., None] * norm_scale).astype(jnp.bfloat16)
    blocked = normed.reshape(steps, block_count, block_rows, -1)
    rank_part = jnp.einsum(
        "tbnd,bdr->tbnr", blocked, query_first, preferred_element_type=jnp.float32
    )
    rank_query = lax.psum(rank_part, ("gx", "gy")).astype(jnp.bfloat16)
    delta_query = jnp.einsum(
        "tbnr,bre->tbne", rank_query, query_second, preferred_element_type=jnp.float32
    ).reshape(steps, request_count, -1)
    part_query = (
        jnp.einsum("tnd,de->tne", normed, query_weight, preferred_element_type=jnp.float32)
        + delta_query
    )
    part_key = jnp.einsum("tnd,de->tne", normed, key_weight, preferred_element_type=jnp.float32)
    part_value = jnp.einsum("tnd,de->tne", normed, value_weight, preferred_element_type=jnp.float32)
    joined = jnp.concatenate([part_query, part_key, part_value], axis=-1)
    summed = lax.psum_scatter(joined, "gx", scatter_dimension=1, tiled=True).astype(jnp.bfloat16)
    chunk_rows = summed.shape[1] // across_second
    spread = lax.all_to_all(
        summed.reshape(steps, across_second, chunk_rows, -1), "gy", 1, 2, tiled=False
    )
    query_full = spread[..., :query_width].reshape(steps, local_rows, -1)
    key_full = spread[..., query_width : query_width + key_width].reshape(steps, local_rows, -1)
    value_full = spread[..., query_width + key_width :].reshape(steps, local_rows, -1)
    token_positions = (
        cache_lengths[None, :] + jnp.arange(steps, dtype=jnp.int32)[:, None]
    ).reshape(-1)
    query_rot = rotary_embedding(
        query_full.astype(jnp.float32).reshape(steps * local_rows, QUERY_HEADS, HEAD_FEATURES),
        token_positions,
    ).astype(jnp.bfloat16)
    key_rot = rotary_embedding(
        key_full.astype(jnp.float32).reshape(steps * local_rows, KEY_VALUE_HEADS, HEAD_FEATURES),
        token_positions,
    ).astype(jnp.bfloat16)
    mixed_local = attend(
        query_rot.reshape(steps, local_rows, -1),
        cache_keys,
        cache_values,
        key_rot.reshape(steps, local_rows, -1),
        value_full,
        cache_lengths,
    )
    head_group = lax.all_to_all(
        mixed_local.reshape(steps, local_rows, across_second, -1), "gy", 2, 1, tiled=False
    ).reshape(steps, across_second * local_rows, -1)
    mixed_all = lax.all_gather(head_group, "gx", axis=1, tiled=True)
    rank_part_out = jnp.einsum(
        "tbnq,bqr->tbnr",
        mixed_all.reshape(steps, block_count, block_rows, -1),
        output_first,
        preferred_element_type=jnp.float32,
    )
    rank_output = lax.psum(rank_part_out, ("gx", "gy")).astype(jnp.bfloat16)
    delta_output = jnp.einsum(
        "tbnr,bre->tbne", rank_output, output_second, preferred_element_type=jnp.float32
    ).reshape(steps, request_count, -1)
    partial_out = (
        jnp.einsum("tnq,qe->tne", mixed_all, output_weight, preferred_element_type=jnp.float32)
        + delta_output
    )
    return lax.psum_scatter(partial_out, "gy", scatter_dimension=1, tiled=True).astype(jnp.bfloat16)


def solution(mesh):
    in_specs = (
        P(None, "gy", "gx"),
        P("gx"),
        P("gx", "gy"),
        P("gx", "gy"),
        P("gx", "gy"),
        P("gy", "gx"),
        P("gy", "gx", None),
        P("gx", None, "gy"),
        P("gx", "gy", None),
        P("gy", None, "gx"),
        P(),
        P(("gx", "gy")),
        P(("gx", "gy"), None, None),
        P(("gx", "gy"), None, None),
    )
    out_specs = P(None, "gy", "gx")
    return jax.shard_map(local, mesh=mesh, in_specs=in_specs, out_specs=out_specs, check_vma=False)
```

profile of v0, /device:TPU:0, one launch (start us, length us, event | category | flops | bytes accessed | tf_op | source)
XLA Modules:
  0.0 441.3 jit_solution(3828490205044012605)
XLA Ops:
  7.3 1.4 fusion.85
  15.6 1.1 dynamic-slice_select_fusion.3
  16.7 14.6 %all-gather.3.cloned.1.call-done = bf16[3,256,1024]{2,1,0:T(8,128)(2,1)} async-done(((bf16[3,64,1024]{2,1,0:T(8,128)(2,1)}), bf16[3,256,1024]{2,1,0:T(8,128)(2,1)}) %all-gather.3.cloned.1.call-update) | async-done | bytes 1572880 | tf_op jit(solution)/shard_map/all_gather | solution.py:139
  31.3 1.8 fusion.12
  33.1 21.4 %psum.21 = f32[3,256]{1,0:T(4,128)S(1)} all-reduce(f32[3,256]{1,0:T(4,128)S(1)} %fusion.12), channel_id=1, replica_groups=mesh['gx'=8,'gy'=4] {'gx'}, use_global_device_ids=true, to_apply=%region_1.2 | all-reduce | flops 768 | bytes 6144 | tf_op jit(solution)/shard_map/psum | solution.py:141
  54.5 1.8 fusion.14
  56.9 39.3 %all-reduce.2 = bf16[3,2,128,64]{2,3,0,1:T(8,128)(2,1)S(1)} all-reduce(f32[3,2,128,64]{2,3,0,1:T(8,128)S(1)} %fusion.28), channel_id=1, replica_groups=mesh['gx'=8,'gy'=4] {'gx','gy'}, use_global_device_ids=true, to_apply=%region_2.3 | all-reduce | flops 49152 | bytes 294912 | tf_op jit(solution)/shard_map/psum | solution.py:148
  100.3 3.5 bitcast_add_fusion
  103.8 3.5 pad_maximum_fusion
  108.1 139.1 %reduce-scatter.3.cloned.1.call-done = f32[3,32,2560]{2,1,0:T(8,128)} async-done(((f32[3,256,2560]{2,1,0:T(8,128)}), f32[3,32,2560]{2,1,0:T(8,128)}) %reduce-scatter.3.cloned.1.call-update) | async-done | bytes 983056 | tf_op jit(solution)/shard_map/reduce_scatter | solution.py:159
  247.1 1.3 convert_bitcast_fusion
  249.2 3.5 all-to-all-start
  253.1 8.0 %all-to-all-done = bf16[3,4,8,1,2560]{4,2,0,3,1:T(8,128)(2,1)S(1)} async-done(((bf16[3,4,8,1,2560]{4,2,0,3,1:T(8,128)(2,1)}), bf16[3,4,8,1,2560]{4,2,0,3,1:T(8,128)(2,1)S(1)}, u32[]{:S(2)}, u32[]{:S(2)}) %all-to-all-start) | async-done | bytes 491552 | tf_op jit(solution)/shard_map/all_to_all | solution.py:161
  262.8 4.6 %fusion.86 = (f32[8,8,24]{2,1,0:T(8,128)S(1)}, f32[8,8,24,256]{3,2,1,0:T(8,128)S(1)}) fusion(pred[8,256]{1,0:T(8,128)(4,1)S(1)} %iota_compare_fusion, bf16[8,256,1024]{2,1,0:T(8,128)(2,1)} %param.26, bf16[3,8,8,8,64]{4,3,2,1,0:T(8,128)(2,1)S(1)} %bitcast.137, bf16[3,8,8,8,64]{4,3,2,1,0:T(8,128)(2,1)S(1)} %bitcast.135), kind=kOutput, calls=%fused_computation.111 | convolution fusion | flops 102627840 | bytes 6168576 | tf_op jit(solution)/shard_map/rhqd,rchd->rhqc/dot_general | solution.py:62
  269.1 3.1 fusion.41
  272.6 9.8 %all_to_all.30 = bf16[3,1,8,4,2048]{4,2,0,1,3:T(8,128)(2,1)S(1)} all-to-all(bf16[3,1,8,4,2048]{4,2,0,1,3:T(8,128)(2,1)S(1)} %copy.55), channel_id=1, replica_groups=mesh['gx'=8,'gy'=4] {'gy'}, dimensions={3} | all-to-all | bytes 786432 | tf_op jit(solution)/shard_map/all_to_all | solution.py:186
  284.3 1.1 dynamic-slice_select_fusion.1
  285.4 56.7 %all-gather.5.cloned.1.call-done = bf16[3,256,2048]{2,1,0:T(8,128)(2,1)} async-done(((bf16[3,32,2048]{2,1,0:T(8,128)(2,1)}), bf16[3,256,2048]{2,1,0:T(8,128)(2,1)}) %all-gather.5.cloned.1.call-update) | async-done | bytes 3145744 | tf_op jit(solution)/shard_map/all_gather | solution.py:189
  342.1 3.0 fusion.31
  345.1 42.6 %all-reduce.3 = bf16[3,2,128,64]{2,3,0,1:T(8,128)(2,1)S(1)} all-reduce(f32[3,2,128,64]{2,3,0,1:T(8,128)S(1)} %fusion.31), channel_id=1, replica_groups=mesh['gx'=8,'gy'=4] {'gx','gy'}, use_global_device_ids=true, to_apply=%region_8.9 | all-reduce | flops 49152 | bytes 294912 | tf_op jit(solution)/shard_map/psum | solution.py:196
  389.5 1.4 copy-done.5
  390.9 5.1 %bitcast_add_fusion.1 = f32[3,256,1024]{2,1,0:T(8,128)} fusion(f32[3,2,128,1024]{3,2,1,0:T(8,128)S(1)} %copy.58, bf16[3,256,2048]{2,1,0:T(8,128)(2,1)S(1)} %copy-done.6, bf16[2048,1024]{1,0:T(8,128)(2,1)S(1)} %copy-done.5), kind=kOutput, calls=%fused_computation.18 | convolution fusion | flops 3222011904 | bytes 13631488 | tf_op jit(solution)/shard_map/tnq,qe->tne/dot_general | solution.py:201
  396.1 36.8 %reduce-scatter.5.cloned.1.call-done = f32[3,64,1024]{2,1,0:T(8,128)} async-done(((f32[3,256,1024]{2,1,0:T(8,128)}), f32[3,64,1024]{2,1,0:T(8,128)}) %reduce-scatter.5.cloned.1.call-update) | async-done | bytes 786448 | tf_op jit(solution)/shard_map/reduce_scatter | solution.py:204
  432.8 1.9 convert_element_type.74
  (62 shorter events, 16.4 us)
Async XLA Ops:
  6.5 91.5 %copy-start = (bf16[1024,256]{1,0:T(8,128)(2,1)S(1)}, bf16[1024,256]{1,0:T(8,128)(2,1)}, u32[]{:S(2)}) copy-start(bf16[1024,256]{1,0:T(8,128)(2,1)} %param.18) | copy-start | bytes 1572868
  6.5 24.8 %all-gather.3.cloned.1.call-start = ((), (), s32[]{:S(2)}) async-start(), calls=%async_computation.4 | async-start | bytes 1966080 | tf_op jit(solution)/shard_map/all_gather | solution.py:139
  7.3 239.9 %reduce-scatter.3.cloned.1.call-start = ((), (), s32[]{:S(2)}) async-start(), calls=%async_computation.5 | async-start | bytes 8847360 | tf_op jit(solution)/shard_map/reduce_scatter | solution.py:159
  97.3 1.4 copy-start.2
  98.1 2.2 copy-start.4
  107.3 0.7 copy-start.3
  249.2 11.9 %all-to-all-start = ((bf16[3,4,8,1,2560]{4,2,0,3,1:T(8,128)(2,1)}), bf16[3,4,8,1,2560]{4,2,0,3,1:T(8,128)(2,1)S(1)}, u32[]{:S(2)}, u32[]{:S(2)}) async-start(bf16[3,4,8,1,2560]{4,2,0,3,1:T(8,128)(2,1)} %copy.44), calls=%async_computation.1 | async-start | bytes 983040 | tf_op jit(solution)/shard_map/all_to_all | solution.py:161
  252.7 89.4 %all-gather.5.cloned.1.call-start = ((), (), s32[]{:S(2)}) async-start(), calls=%async_computation.6 | async-start | bytes 3538944 | tf_op jit(solution)/shard_map/all_gather | solution.py:189
  283.2 149.6 %reduce-scatter.5.cloned.1.call-start = ((), (), s32[]{:S(2)}) async-start(), calls=%async_computation.7 | async-start | bytes 3932160 | tf_op jit(solution)/shard_map/reduce_scatter | solution.py:204
  387.6 1.9 copy-start.6
  388.3 2.7 copy-start.5
  390.9 43.8 %copy-start.1 = (bf16[1024,256]{1,0:T(8,128)(2,1)S(1)}, bf16[1024,256]{1,0:T(8,128)(2,1)}, u32[]{:S(2)}) copy-start(bf16[1024,256]{1,0:T(8,128)(2,1)} %param.18) | copy-start | bytes 1572868
Sparse Core Ops, SparseCore 0:
  8.9 22.3 all-gather.2
  107.5 139.6 reduce-scatter.2
  283.4 58.6 all-gather.4
  396.2 36.6 reduce-scatter.4
where the time goes:
time: 442 us; the launch traced here: 441 us
  waiting for transfers between devices  256 us (58%)
  blocking collectives  113 us (26%)
  matrix products  23.5 us (5%)
  between operations  18.7 us (4%)
  other arithmetic  16.6 us (4%)
  local copies, waits for them, and re-layouts  9.71 us (2%)
    reduce_scatter x1, waiting for transfers between devices, local(): lax.psum_scatter(joined, 'gx', scatter_dimension=1, tiled=True)  139 us
    all_gather x1, waiting for transfers between devices, local(): mixed_all = lax.all_gather(head_group, 'gx', axis=1, tiled=True)  56.7 us
    psum x1, blocking collectives, local(): rank_output = lax.psum(rank_part_out, ('gx', 'gy')).astype(jnp.bfloat16)  42.6 us
    psum x1, blocking collectives, local(): rank_query = lax.psum(rank_part, ('gx', 'gy')).astype(jnp.bfloat16)  39.3 us
    reduce_scatter x1, waiting for transfers between devices, local(): lax.psum_scatter(partial_out, 'gy', scatter_dimension=1, tiled=True)  36.8 us
    psum x1, blocking collectives, local(): squares = lax.psum(jnp.sum(rows_wide * rows_wide, axis=2), 'gx')  21.4 us
    all_gather x1, waiting for transfers between devices, local(): rows_all = lax.all_gather(inputs, 'gy', axis=1, tiled=True)  14.6 us
    all_to_all x1, blocking collectives, local(): lax.all_to_all(mixed_local.reshape(steps, local_rows, across_second, -1),...  9.84 us
  transfers between devices with their start and end apart: 5, of which 5 were waited for; matrix products, arithmetic and copies ran while one was open for 1% of the time, Pallas kernels for 0%

commit v1 on v0

--- a/solution.py
+++ b/solution.py
@@ -145,7 +145,7 @@
     rank_part = jnp.einsum(
         "tbnd,bdr->tbnr", blocked, query_first, preferred_element_type=jnp.float32
     )
-    rank_query = lax.psum(rank_part, ("gx", "gy")).astype(jnp.bfloat16)
+    rank_query = lax.psum(lax.psum(rank_part, "gy"), "gx").astype(jnp.bfloat16)
     delta_query = jnp.einsum(
         "tbnr,bre->tbne", rank_query, query_second, preferred_element_type=jnp.float32
     ).reshape(steps, request_count, -1)

time: 442 us -> 467 us (1.057)
  waiting for transfers between devices: 256 us -> 278 us
    psum x0 -> x1, waiting for transfers between devices: none -> 25 us  [local(): rank_query = lax.psum(lax.psum(rank_part, 'gy'), 'gx').astype(jnp.bfloat16)]
  transfers between devices with their start and end apart: 5 -> 6, of which waited for: 5 -> 6; matrix products, arithmetic and copies ran while one was open for 1% -> 2% of each run, Pallas kernels for 0% -> 0%
where the time goes in v1:
time: 467 us; the launch traced here: 466 us
  waiting for transfers between devices  278 us (60%)
  blocking collectives  113 us (24%)
  matrix products  26.1 us (6%)
  between operations  18.7 us (4%)
  other arithmetic  16.6 us (4%)
  local copies, waits for them, and re-layouts  10.1 us (2%)
    reduce_scatter x1, waiting for transfers between devices, local(): lax.psum_scatter(joined, 'gx', scatter_dimension=1, tiled=True)  136 us
    all_gather x1, waiting for transfers between devices, local(): mixed_all = lax.all_gather(head_group, 'gx', axis=1, tiled=True)  56.8 us
    psum x1, blocking collectives, local(): rank_output = lax.psum(rank_part_out, ('gx', 'gy')).astype(jnp.bfloat16)  42.6 us
    psum x1, blocking collectives, local(): rank_query = lax.psum(lax.psum(rank_part, 'gy'), 'gx').astype(jnp.bfloat16)  39.7 us
    reduce_scatter x1, waiting for transfers between devices, local(): lax.psum_scatter(partial_out, 'gy', scatter_dimension=1, tiled=True)  36.8 us
    psum x1, waiting for transfers between devices, local(): rank_query = lax.psum(lax.psum(rank_part, 'gy'), 'gx').astype(jnp.bfloat16)  25 us
    psum x1, blocking collectives, local(): squares = lax.psum(jnp.sum(rows_wide * rows_wide, axis=2), 'gx')  21.4 us
    all_gather x1, waiting for transfers between devices, local(): rows_all = lax.all_gather(inputs, 'gy', axis=1, tiled=True)  14.6 us
  transfers between devices with their start and end apart: 6, of which 6 were waited for; matrix products, arithmetic and copies ran while one was open for 2% of the time, Pallas kernels for 0%

profile of v1, /device:TPU:0, one launch (start us, length us, event | category | flops | bytes accessed | tf_op | source)
XLA Modules:
  0.0 466.3 jit_solution(8800747580481724320)
XLA Ops:
  7.3 1.4 fusion.85
  16.7 14.6 %all-gather.3.cloned.1.call-done = bf16[3,256,1024]{2,1,0:T(8,128)(2,1)} async-done(((bf16[3,64,1024]{2,1,0:T(8,128)(2,1)}), bf16[3,256,1024]{2,1,0:T(8,128)(2,1)}) %all-gather.3.cloned.1.call-update) | async-done | bytes 1572880 | tf_op jit(solution)/shard_map/all_gather | solution.py:139
  31.3 1.8 fusion.12
  33.1 21.4 %psum.28 = f32[3,256]{1,0:T(4,128)S(1)} all-reduce(f32[3,256]{1,0:T(4,128)S(1)} %fusion.12), channel_id=1, replica_groups=mesh['gx'=8,'gy'=4] {'gx'}, use_global_device_ids=true, to_apply=%region_1.2 | all-reduce | flops 768 | bytes 6144 | tf_op jit(solution)/shard_map/psum | solution.py:141
  54.5 1.8 fusion.14
  58.3 2.5 fusion.54
  60.8 25.0 %all-reduce.4.cloned.1.call-done = f32[3,2,128,64]{2,3,0,1:T(8,128)} async-done(((f32[3,2,128,64]{2,3,0,1:T(8,128)}), f32[3,2,128,64]{2,3,0,1:T(8,128)}) %all-reduce.4.cloned.1.call-update) | async-done | bytes 196624 | tf_op jit(solution)/shard_map/psum | solution.py:148
  85.8 39.7 %all-reduce.5 = bf16[3,2,128,64]{2,3,0,1:T(8,128)(2,1)S(1)} all-reduce(f32[3,2,128,64]{2,3,0,1:T(8,128)} %all-reduce.4.cloned.1.call-done), channel_id=1, replica_groups=mesh['gx'=8,'gy'=4] {'gx'}, use_global_device_ids=true, to_apply=%region_3.4 | all-reduce | flops 49152 | bytes 294912 | tf_op jit(solution)/shard_map/psum | solution.py:148
  127.3 1.4 copy-done.4
  128.7 3.5 bitcast_add_fusion
  132.2 3.5 pad_maximum_fusion
  136.4 135.7 %reduce-scatter.3.cloned.1.call-done = f32[3,32,2560]{2,1,0:T(8,128)} async-done(((f32[3,256,2560]{2,1,0:T(8,128)}), f32[3,32,2560]{2,1,0:T(8,128)}) %reduce-scatter.3.cloned.1.call-update) | async-done | bytes 983056 | tf_op jit(solution)/shard_map/reduce_scatter | solution.py:159
  274.2 3.5 all-to-all-start
  278.1 8.0 %all-to-all-done = bf16[3,4,8,1,2560]{4,2,0,3,1:T(8,128)(2,1)S(1)} async-done(((bf16[3,4,8,1,2560]{4,2,0,3,1:T(8,128)(2,1)}), bf16[3,4,8,1,2560]{4,2,0,3,1:T(8,128)(2,1)S(1)}, u32[]{:S(2)}, u32[]{:S(2)}) %all-to-all-start) | async-done | bytes 491552 | tf_op jit(solution)/shard_map/all_to_all | solution.py:161
  287.8 4.6 fusion.86
  294.1 3.1 fusion.41
  297.6 9.8 %all_to_all.30 = bf16[3,1,8,4,2048]{4,2,0,1,3:T(8,128)(2,1)S(1)} all-to-all(bf16[3,1,8,4,2048]{4,2,0,1,3:T(8,128)(2,1)S(1)} %copy.55), channel_id=1, replica_groups=mesh['gx'=8,'gy'=4] {'gy'}, dimensions={3} | all-to-all | bytes 786432 | tf_op jit(solution)/shard_map/all_to_all | solution.py:186
  310.4 56.8 %all-gather.5.cloned.1.call-done = bf16[3,256,2048]{2,1,0:T(8,128)(2,1)} async-done(((bf16[3,32,2048]{2,1,0:T(8,128)(2,1)}), bf16[3,256,2048]{2,1,0:T(8,128)(2,1)}) %all-gather.5.cloned.1.call-update) | async-done | bytes 3145744 | tf_op jit(solution)/shard_map/all_gather | solution.py:189
  367.1 3.0 fusion.31
  370.1 42.6 %all-reduce.6 = bf16[3,2,128,64]{2,3,0,1:T(8,128)(2,1)S(1)} all-reduce(f32[3,2,128,64]{2,3,0,1:T(8,128)S(1)} %fusion.31), channel_id=1, replica_groups=mesh['gx'=8,'gy'=4] {'gx','gy'}, use_global_device_ids=true, to_apply=%region_9.10 | all-reduce | flops 49152 | bytes 294912 | tf_op jit(solution)/shard_map/psum | solution.py:196
  414.6 1.4 copy-done.5
  416.0 5.1 %bitcast_add_fusion.1 = f32[3,256,1024]{2,1,0:T(8,128)} fusion(f32[3,2,128,1024]{3,2,1,0:T(8,128)S(1)} %copy.58, bf16[3,256,2048]{2,1,0:T(8,128)(2,1)S(1)} %copy-done.6, bf16[2048,1024]{1,0:T(8,128)(2,1)S(1)} %copy-done.5), kind=kOutput, calls=%fused_computation.18 | convolution fusion | flops 3222011904 | bytes 13631488 | tf_op jit(solution)/shard_map/tnq,qe->tne/dot_general | solution.py:201
  421.1 36.8 %reduce-scatter.5.cloned.1.call-done = f32[3,64,1024]{2,1,0:T(8,128)} async-done(((f32[3,256,1024]{2,1,0:T(8,128)}), f32[3,64,1024]{2,1,0:T(8,128)}) %reduce-scatter.5.cloned.1.call-update) | async-done | bytes 786448 | tf_op jit(solution)/shard_map/reduce_scatter | solution.py:204
  457.8 1.9 convert_element_type.74
  (65 shorter events, 18.9 us)
Async XLA Ops:
  6.5 51.1 %copy-start = (bf16[1024,256]{1,0:T(8,128)(2,1)S(1)}, bf16[1024,256]{1,0:T(8,128)(2,1)}, u32[]{:S(2)}) copy-start(bf16[1024,256]{1,0:T(8,128)(2,1)} %param.18) | copy-start | bytes 1572868
  6.5 24.8 %all-gather.3.cloned.1.call-start = ((), (), s32[]{:S(2)}) async-start(), calls=%async_computation.4 | async-start | bytes 1966080 | tf_op jit(solution)/shard_map/all_gather | solution.py:139
  7.3 78.5 %all-reduce.4.cloned.1.call-start = ((), (), s32[]{:S(2)}) async-start(), calls=%async_computation.5 | async-start | bytes 393216 | tf_op jit(solution)/shard_map/psum | solution.py:148
  57.6 214.5 %reduce-scatter.3.cloned.1.call-start = ((), (), s32[]{:S(2)}) async-start(), calls=%async_computation.6 | async-start | bytes 8847360 | tf_op jit(solution)/shard_map/reduce_scatter | solution.py:159
  126.5 2.2 copy-start.4
  128.7 3.5 copy-start.2
  135.7 0.7 copy-start.3
  274.2 11.9 %all-to-all-start = ((bf16[3,4,8,1,2560]{4,2,0,3,1:T(8,128)(2,1)}), bf16[3,4,8,1,2560]{4,2,0,3,1:T(8,128)(2,1)S(1)}, u32[]{:S(2)}, u32[]{:S(2)}) async-start(bf16[3,4,8,1,2560]{4,2,0,3,1:T(8,128)(2,1)} %copy.44), calls=%async_computation.1 | async-start | bytes 983040 | tf_op jit(solution)/shard_map/all_to_all | solution.py:161
  277.7 89.5 %all-gather.5.cloned.1.call-start = ((), (), s32[]{:S(2)}) async-start(), calls=%async_computation.7 | async-start | bytes 3538944 | tf_op jit(solution)/shard_map/all_gather | solution.py:189
  308.2 149.6 %reduce-scatter.5.cloned.1.call-start = ((), (), s32[]{:S(2)}) async-start(), calls=%async_computation.8 | async-start | bytes 3932160 | tf_op jit(solution)/shard_map/reduce_scatter | solution.py:204
  412.7 1.9 copy-start.6
  413.3 2.7 copy-start.5
  416.0 43.8 %copy-start.1 = (bf16[1024,256]{1,0:T(8,128)(2,1)S(1)}, bf16[1024,256]{1,0:T(8,128)(2,1)}, u32[]{:S(2)}) copy-start(bf16[1024,256]{1,0:T(8,128)(2,1)} %param.18) | copy-start | bytes 1572868
Sparse Core Ops, SparseCore 0:
  8.9 22.3 all-gather.2
  57.7 28.0 all-reduce.3
  135.9 136.2 reduce-scatter.2
  308.4 58.7 all-gather.4
  421.2 36.5 reduce-scatter.4
